TPU v7x, 256 devices: a whole 4x4x8 slice. The times are simulated.
256 devices in a mesh: section: 8 (over z), joint: 32 (over y, x, core).
Axes of the slice: x: 4, y: 4, z: 8, core: 2. Of those that a mesh axis runs over, the one named last changes fastest.
Arguments:
- encoder_rows: bfloat16 [32, 1024, 1536], P('joint', 'section'), may hold values from -6 to 6
- up_weight: bfloat16 [1536, 3072], P(None, 'section'), may hold values from -0.15625 to 0.15625
- down_weight: bfloat16 [3072, 1536], P('section'), may hold values from -0.109375 to 0.109375
- encoder_proj: bfloat16 [1536, 640], replicated, may hold values from -0.15625 to 0.15625
- embedding: bfloat16 [4096, 640], P('joint'), may hold values from -6 to 6
- conv_taps: float32 [2, 640], replicated, may hold values from -3 to 3
- decoder_proj: bfloat16 [640, 640], replicated, may hold values from -0.25 to 0.25
- output_proj: bfloat16 [640, 4096], replicated, may hold values from -0.5 to 0.5
- output_bias: float32 [4096], replicated, may hold values from -6 to 6
- frame_lengths: int32 [32], replicated, may hold values from 1 to 1024, 20480 in all
- label_lengths: int32 [32], replicated, may hold values from 1 to 3, 48 in all
- label_ids: int32 [32, 3], replicated, may hold values from 1 to 4095
- owner_index: int32 [32], replicated, may hold values from 0 to 31, each once
Outputs:
- enc_grad: bfloat16 [32, 1024, 1536], P('joint', 'section')
- up_grad: float32 [1536, 3072], P('joint', 'section')
- down_grad: float32 [3072, 1536], P('section', 'joint')
- pred_grad: float32 [32, 4, 640], P('joint', None, 'section')
Inputs may be any that keep to these rules, and one draw needn't show every extreme that they name: `owner_index`: every joint owner receives exactly one utterance. `frame_lengths`: the longest utterance uses all 1024 frames. `label_lengths`: the longest label sequence has 3 labels. `label_ids`: never the blank token 0.
All inputs are finite; a program needn't handle non-finite values.
Results may differ from a plain program's by a relative error of at most 0.013.
Values may be sent and summed in bfloat16 or wider, within the bound.
No kernel may reach another device: no remote copies, remote signals or barrier semaphores. Data moves between devices by JAX's collectives and lax.ppermute only.
A program may use at most 128 MiB of HBM per device.

v0:
```python
import jax
import jax.numpy as jnp
from jax import lax
from jax.sharding import PartitionSpec as P

NEG_BIG = -1000000000.0


def partner_2(block, axis, bit):
    count = lax.axis_size(axis)
    route = []
    for low in range(count):
        high = low | 1 << bit
        if high != low and high < count:
            route += [(low, high), (high, low)]
    return lax.ppermute(block, axis, route)


def from_behind(value, axis, steps):
    count = lax.axis_size(axis)
    initial, last = (max(0, -steps), min(count, count - steps))
    return lax.ppermute(value, axis, [(source, source + steps) for source in range(initial, last)])


def layer_norm(values):
    average = jnp.mean(values, axis=-1, keepdims=True)
    centered = values - average
    variance = jnp.mean(centered * centered, axis=-1, keepdims=True)
    inv_scale = lax.rsqrt(variance + 1e-05)
    return (centered * inv_scale, inv_scale)


def lower_paths(label_row):
    partial_sums = jnp.concatenate([jnp.zeros((1,), jnp.float32), jnp.cumsum(label_row)])
    places = partial_sums.shape[0]
    row_ids = lax.broadcasted_iota(jnp.int32, (places, places), 0)
    col_ids = lax.broadcasted_iota(jnp.int32, (places, places), 1)
    return jnp.where(col_ids <= row_ids, partial_sums[:, None] - partial_sums[None, :], NEG_BIG)


def advance(vector, blank_row, label_row, active):
    moved = blank_row + jax.nn.logsumexp(lower_paths(label_row) + vector[None, :], axis=1)
    return jnp.where(active, moved, vector)


def run_block(vector, blank_score, label_score, active):

    def run_one_frame(carried, inputs):
        blank_row, label_row, live_flag = inputs
        return (advance(carried, blank_row, label_row, live_flag), None)

    return lax.scan(run_one_frame, vector, (blank_score, label_score, active))[0]


def block_matrix(blank_score, label_score, active):
    places = blank_score.shape[1]
    row_ids = lax.broadcasted_iota(jnp.int32, (places, places), 0)
    col_ids = lax.broadcasted_iota(jnp.int32, (places, places), 1)
    identity_map = jnp.where(row_ids == col_ids, 0.0, NEG_BIG)

    def block_one_frame(carried, inputs):
        blank_row, label_row, live_flag = inputs
        moved = blank_row[:, None] + jax.nn.logsumexp(
            lower_paths(label_row)[:, :, None] + carried[None, :, :], axis=1
        )
        return (jnp.where(live_flag, moved, carried), None)

    return lax.scan(block_one_frame, identity_map, (blank_score, label_score, active))[0]


def log_apply(transfer, vector):
    return jax.nn.logsumexp(transfer + vector[None, :], axis=1)


def log_apply_back(transfer, vector):
    return jax.nn.logsumexp(transfer + vector[:, None], axis=0)


def joint_forward(frame_part, pred_here, label_row_ids, output_proj, output_bias):
    joined = jnp.tanh(frame_part.astype(jnp.float32)[:, None, :] + pred_here[None, :, :]).astype(
        jnp.bfloat16
    )
    frames_here, places, joint_width = joined.shape
    logits = (
        jnp.dot(
            joined.reshape(frames_here * places, joint_width),
            output_proj,
            preferred_element_type=jnp.float32,
        )
        + output_bias
    )
    logits = logits.reshape(frames_here, places, -1)
    exponent = jnp.exp(logits)
    denominator = jnp.sum(exponent, axis=-1, keepdims=True)
    log_total = jnp.log(denominator)[:, :, 0]
    blank_score = logits[:, :, 0] - log_total
    index_grid = jnp.broadcast_to(label_row_ids[None, :, None], (frames_here, places - 1, 1))
    picked = jnp.take_along_axis(logits[:, :-1, :], index_grid, axis=2)[:, :, 0]
    label_score = picked - log_total[:, :-1]
    posterior = exponent / denominator
    return (joined, posterior, blank_score, label_score)


def joint_backward(blank_grad, label_grad, label_row_ids, joined, posterior, output_proj):
    frames_here, places, vocab_size = posterior.shape
    label_full = jnp.pad(label_grad, ((0, 0), (0, 1)))
    weight_sum = blank_grad + label_full
    token_full = jnp.concatenate([label_row_ids, jnp.full((1,), -1, jnp.int32)])
    vocab_iota = lax.broadcasted_iota(jnp.int32, (1, 1, vocab_size), 2)
    blank_term = jnp.where(vocab_iota == 0, blank_grad[:, :, None], 0.0)
    label_term = jnp.where(vocab_iota == token_full[None, :, None], label_full[:, :, None], 0.0)
    logit_grad = -posterior * weight_sum[:, :, None] + blank_term + label_term
    logit_grad = logit_grad.astype(jnp.bfloat16).reshape(frames_here * places, vocab_size)
    joined_grad = lax.dot_general(
        logit_grad, output_proj, (((1,), (1,)), ((), ())), preferred_element_type=jnp.float32
    )
    joined_vals = joined.astype(jnp.float32).reshape(frames_here * places, -1)
    inner_grad = (joined_grad * (1.0 - joined_vals * joined_vals)).reshape(frames_here, places, -1)
    frame_part_grad = jnp.sum(inner_grad, axis=1).astype(jnp.bfloat16)
    pred_part_grad = jnp.sum(inner_grad, axis=0)
    return (frame_part_grad, pred_part_grad)


def network_sections(count):
    sections = []
    block_size = 2
    while block_size <= count:
        stride = block_size // 2
        while stride >= 1:
            sections.append((block_size, stride))
            stride = stride // 2
        block_size = block_size * 2
    return sections


def sort_section(keys, block_size, stride, device_id):
    count = keys.shape[0]
    position = jnp.arange(count, dtype=jnp.int32)
    partner = position ^ stride
    partner_keys = keys[partner]
    rising = position & block_size == 0
    lower_side = position < partner
    keep_small = lower_side == rising
    new_keys = jnp.where(
        keep_small, jnp.minimum(keys, partner_keys), jnp.maximum(keys, partner_keys)
    )
    takes = new_keys[device_id] != keys[device_id]
    return (new_keys, takes)


def route_owner(payload, keys, device_id, count):
    for block_size, stride in network_sections(count):
        keys, takes = sort_section(keys, block_size, stride, device_id)
        other = partner_2(payload, "joint", stride.bit_length() - 1)
        payload = jnp.where(takes, other, payload)
    return payload


def route_holder(payload, keys, device_id, count):
    for block_size, stride in network_sections(count):
        keys, takes = sort_section(keys, block_size, stride, device_id)
        other = partner_2(payload, "joint", stride.bit_length() - 1)
        payload = jnp.where(takes, other, payload)
    return payload


def on_device(
    encoder_rows,
    up_weight,
    down_weight,
    encoder_proj,
    embedding,
    conv_taps,
    decoder_proj,
    output_proj,
    output_bias,
    frame_lengths,
    label_lengths,
    label_ids,
    owner_index,
):
    section_count = lax.axis_size("section")
    joint_count = lax.axis_size("joint")
    section_id = lax.axis_index("section")
    joint_id = lax.axis_index("joint")
    block_len = encoder_rows.shape[1]
    utterances = label_ids.shape[0]
    places = label_ids.shape[1] + 1
    own_rows = encoder_rows[0].astype(jnp.float32)
    normed_in = layer_norm(own_rows)[0].astype(jnp.bfloat16)
    gathered = lax.all_gather(normed_in, "section", axis=0, tiled=True)
    pre_hidden = jnp.dot(gathered, up_weight, preferred_element_type=jnp.float32)
    hidden = jax.nn.silu(pre_hidden).astype(jnp.bfloat16)
    encoded = own_rows + lax.psum_scatter(
        0.5 * jnp.dot(hidden, down_weight, preferred_element_type=jnp.float32),
        "section",
        scatter_dimension=0,
        tiled=True,
    )
    unit_rows, inv_scale = layer_norm(encoded)
    frame_part = jnp.dot(
        unit_rows.astype(jnp.bfloat16), encoder_proj, preferred_element_type=jnp.float32
    ).astype(jnp.bfloat16)
    order_iota = jnp.arange(utterances, dtype=jnp.int32)
    inverse = jnp.zeros((utterances,), jnp.int32).at[owner_index].set(order_iota)
    own_utterance = inverse[joint_id]
    owner_frames = route_owner(frame_part, owner_index, joint_id, joint_count)
    context = jnp.concatenate([jnp.zeros((utterances, 1), jnp.int32), label_ids], axis=1)
    vocab_rows = embedding.shape[0]
    vocab_ids = joint_id * vocab_rows + jnp.arange(vocab_rows, dtype=jnp.int32)

    def label_term(start_row, row_count):
        number = row_count // places
        wanted = context[inverse].reshape(number * places)
        selector = (wanted[:, None] == vocab_ids[None, :]).astype(jnp.bfloat16)
        return jnp.dot(selector, embedding, preferred_element_type=jnp.float32)

    looked = lax.psum_scatter(
        label_term(jnp.int32(0), places * lax.axis_size("joint")).astype(jnp.bfloat16),
        "joint",
        scatter_dimension=0,
        tiled=True,
    ).astype(jnp.float32)
    previous = jnp.concatenate([looked[:1], looked[:-1]], axis=0)
    pred_act = jnp.maximum(conv_taps[0] * previous + conv_taps[1] * looked, 0.0).astype(
        jnp.bfloat16
    )
    pred_rows = jnp.dot(pred_act, decoder_proj, preferred_element_type=jnp.float32)
    label_here = label_ids[own_utterance]
    frames_used = frame_lengths[own_utterance]
    labels_used = label_lengths[own_utterance]
    joined, posterior, blank_score, label_score = joint_forward(
        owner_frames, pred_rows, label_here, output_proj, output_bias
    )
    frame_ids = section_id * block_len + jnp.arange(block_len, dtype=jnp.int32)
    active = frame_ids < frames_used
    transfer = block_matrix(blank_score, label_score, active)
    place_iota = jnp.arange(places, dtype=jnp.int32)
    start_vec = jnp.where(place_iota == 0, 0.0, NEG_BIG)
    finish_vec = jnp.where(place_iota == labels_used, 0.0, NEG_BIG)

    def forward_turn(turn_index, carried):
        passed = from_behind(log_apply(transfer, carried), "section", 1)
        return jnp.where(section_id == 0, start_vec, passed)

    incoming = lax.fori_loop(0, section_count - 1, forward_turn, start_vec)

    def backward_turn(turn_index, carried):
        passed = from_behind(log_apply_back(transfer, carried), "section", -1)
        return jnp.where(section_id == section_count - 1, finish_vec, passed)

    leaving = lax.fori_loop(0, section_count - 1, backward_turn, finish_vec)

    def block_out(blank_in, label_in):
        return run_block(incoming, blank_in, label_in, active)

    end_alpha, pullback = jax.vjp(block_out, blank_score, label_score)
    logprob = jax.nn.logsumexp(end_alpha + leaving)
    blank_grad, label_grad = pullback(-jnp.exp(end_alpha + leaving - logprob))
    frame_part_grad, pred_part = joint_backward(
        blank_grad, label_grad, label_here, joined, posterior, output_proj
    )
    part_grad = route_holder(frame_part_grad, inverse, joint_id, joint_count)
    unit_grad = lax.dot_general(
        part_grad, encoder_proj, (((1,), (1,)), ((), ())), preferred_element_type=jnp.float32
    )
    first_mean = jnp.mean(unit_grad, axis=-1, keepdims=True)
    second_mean = jnp.mean(unit_grad * unit_rows, axis=-1, keepdims=True)
    row_grad = (inv_scale * (unit_grad - first_mean - unit_rows * second_mean)).astype(jnp.bfloat16)
    grad_all = lax.all_gather(row_grad, "section", axis=0, tiled=True)
    hidden_grad = 0.5 * lax.dot_general(
        grad_all, down_weight, (((1,), (1,)), ((), ())), preferred_element_type=jnp.float32
    )
    gate_sigmoid = jax.nn.sigmoid(pre_hidden)
    pre_grad = (hidden_grad * gate_sigmoid * (1.0 + pre_hidden * (1.0 - gate_sigmoid))).astype(
        jnp.bfloat16
    )
    up_part = lax.dot_general(
        gathered, pre_grad, (((0,), (0,)), ((), ())), preferred_element_type=jnp.float32
    )
    down_part = 0.5 * lax.dot_general(
        hidden, grad_all, (((0,), (0,)), ((), ())), preferred_element_type=jnp.float32
    )
    up_sum, down_sum = (
        lax.psum_scatter(
            up_part.astype(jnp.bfloat16), "joint", scatter_dimension=0, tiled=True
        ).astype(jnp.float32),
        lax.psum_scatter(
            down_part.astype(jnp.bfloat16), "joint", scatter_dimension=1, tiled=True
        ).astype(jnp.float32),
    )
    pred_sum = lax.psum_scatter(pred_part[None], "section", scatter_dimension=2, tiled=True)
    return (row_grad[None], up_sum, down_sum, pred_sum)


def solution(mesh):
    return jax.shard_map(
        on_device,
        mesh=mesh,
        in_specs=(
            P("joint", "section", None),
            P(None, "section"),
            P("section", None),
            P(),
            P("joint", None),
            P(),
            P(),
            P(),
            P(),
            P(),
            P(),
            P(),
            P(),
        ),
        out_specs=(
            P("joint", "section", None),
            P("joint", "section"),
            P("section", "joint"),
            P("joint", None, "section"),
        ),
        check_vma=False,
    )
```

profile of v0, /device:TPU:2, one launch (start us, length us, event | category | flops | bytes accessed | tf_op | source)
XLA Modules:
  0.0 2108.3 jit_solution(6235568972007815648)
XLA Ops:
  12.7 48.0 %all-gather.3.cloned.1.call-done = bf16[1024,1536]{1,0:T(8,128)(2,1)} async-done(((bf16[128,1536]{1,0:T(8,128)(2,1)}), bf16[1024,1536]{1,0:T(8,128)(2,1)}) %all-gather.3.cloned.1.call-update) | async-done | bytes 3145744 | tf_op jit(solution)/shard_map/all_gather | solution.py:191
  60.7 3.8 fusion.93
  65.7 4.5 convolution_multiply_fusion
  86.9 57.3 %reduce-scatter.7.cloned.1.call-done = f32[128,1536]{1,0:T(8,128)} async-done(((f32[1024,1536]{1,0:T(8,128)}), f32[128,1536]{1,0:T(8,128)}) %reduce-scatter.7.cloned.1.call-update) | async-done | bytes 786448 | tf_op jit(solution)/shard_map/reduce_scatter | solution.py:194
  164.8 3.2 collective-permute-done.5
  179.8 5.0 collective-permute-done.8
  184.8 2.8 collective-permute-start.9
  188.3 3.6 collective-permute-done.9
  200.3 3.0 collective-permute-start.12
  229.0 3.5 broadcast_in_dim.222
  232.5 6.8 broadcast_in_dim.223
  246.4 9.4 exponential_reduce_fusion.3
  255.9 9.8 reshape.609
  266.7 5.5 gather_fusion.31
  275.0 308.2 %while.74 = (s32[]{:T(128)}, f32[4,4]{1,0:T(4,128)S(1)}, pred[128]{0:T(512)(128)(4,1)S(1)}, f32[128,4]{1,0:T(8,128)S(1)}, f32[128,3]{1,0:T(8,128)}, /*index=5*/s32[]{:T(128)}, f32[]{:T(128)}, f32[1]{0:T(128)}) while((s32[]{:T(128)}, f32[4,4]{1,0:T(4,128)S(1)}, pred[128]{0:T(512)(128)(4,1)S(1)}, f32[128,4]{1,0:T(8,128)S(1)}, ...), condition=%wide.region_12.13_spmd, body=%wide.region_8.0_spmd.sunk | while | flops 476 | bytes 1144 | solution.py:68
  583.2 39.8 %while.75 = (s32[]{:T(128)}, f32[4]{0:T(128)S(1)}, pred[]{:T(512)}, f32[4,4]{1,0:T(4,128)S(1)}, s32[]{:T(128)}) while((s32[]{:T(128)}, f32[4]{0:T(128)S(1)}, pred[]{:T(512)}, f32[4,4]{1,0:T(4,128)S(1)}, s32[]{:T(128)}) %tuple.157), condition=%wide.region_16.17_spmd.clone, body=%wide.region_13.16_spmd.clone.sunk | while | flops 110 | bytes 486 | solution.py:246
  586.8 4.2 collective-permute-start
  592.6 4.2 collective-permute-start
  598.4 4.2 collective-permute-start
  604.2 4.2 collective-permute-start
  610.0 4.7 collective-permute-start
  616.3 5.4 collective-permute-start
  623.0 567.5 %while.78 = (s32[]{:T(128)}, f32[4]{0:T(128)S(1)}, f32[128,4,4]{2,1,0:T(4,128)}, pred[128,4]{1,0:T(8,128)(4,1)}, f32[128,4]{1,0:T(8,128)S(1)}, /*index=5*/pred[1...) while((s32[]{:T(128)}, f32[4]{0:T(128)S(1)}, ...), condition=%wide.region_21.22_spmd.clone.clone, body=%wide.region_17.21_spmd.clone.clone.sunk | while | flops 296 | bytes 5132 | solution.py:52
  1190.5 53.7 %while.76 = (s32[]{:T(128)}, f32[4]{0:T(128)S(1)}, pred[]{:T(512)}, f32[4,4]{1,0:T(4,128)S(1)}, s32[]{:T(128)}, /*index=5*/s32[]{:T(128)}) while((s32[]{:T(128)}, f32[4]{0:T(128)S(1)}, pred[]{:T(512)}, f32[4,4]{1,0:T(4,128)S(1)}, s32[]{:T(128)}, /*index=5*/s32[]{:T(128)}) %tuple.183), condition=%wide.region_25.26_spmd.clone, body=%wide.region_22.25_spmd.clone.sunk | while | flops 110 | bytes 498 | solution.py:252
  1192.0 5.6 collective-permute-done.1
  1199.7 5.6 collective-permute-done.1
  1207.5 5.6 collective-permute-done.1
  1215.3 5.6 collective-permute-done.1
  1223.1 5.4 collective-permute-done.1
  1230.6 5.4 collective-permute-done.1
  1238.1 5.4 collective-permute-done.1
  1247.4 484.2 %while.77 = (s32[]{:T(128)}, f32[4]{0:T(128)S(1)}, f32[128,4]{1,0:T(8,128)S(1)}, f32[128,3]{1,0:T(8,128)S(1)}, pred[128]{0:T(512)(128)(4,1)S(1)}, /*index=5*/pre...) while((s32[]{:T(128)}, f32[4]{0:T(128)S(1)}, ...), condition=%wide.region_33.34_spmd.clone, body=%wide.region_28.33_spmd.clone.sunk | while | flops 133 | bytes 553 | solution.py:52
  1731.9 12.4 fusion.31
  1744.3 2.8 reshape.610
  1755.9 3.0 collective-permute-done.18
  1766.4 4.6 collective-permute-done.20
  1774.7 2.7 collective-permute-done.21
  1780.2 3.1 collective-permute-start.23
  1788.3 5.2 collective-permute-start.24
  1801.2 3.2 collective-permute-done.25
  1812.6 3.7 collective-permute-done.27
  1822.1 5.0 collective-permute-start.29
  1843.2 49.4 %all-gather.5.cloned.1.call-done = bf16[1024,1536]{1,0:T(8,128)(2,1)} async-done(((bf16[128,1536]{1,0:T(8,128)(2,1)}), bf16[1024,1536]{1,0:T(8,128)(2,1)}) %all-gather.5.cloned.1.call-update) | async-done | bytes 3145744 | tf_op jit(solution)/shard_map/all_gather | solution.py:270
  1892.6 5.3 fusion.30
  1898.0 7.8 convolution_convert_fusion
  1905.8 25.1 %reduce-scatter.13.cloned.1.call-done = f32[80,4]{1,0:T(8,128)} async-done(((f32[640,4]{1,0:T(8,128)}), f32[80,4]{1,0:T(8,128)}) %reduce-scatter.13.cloned.1.call-update) | async-done | bytes 1296
  1932.3 82.1 %reduce-scatter.11.cloned.1.call-done = bf16[384,48]{0,1:T(8,128)(2,1)} async-done(((bf16[384,1536]{0,1:T(8,128)(2,1)}), bf16[384,48]{0,1:T(8,128)(2,1)}) %reduce-scatter.11.cloned.1.call-update) | async-done | bytes 36880 | tf_op jit(solution)/shard_map/reduce_scatter | solution.py:288
  2015.8 83.2 %reduce-scatter.9.cloned.1.call-done = bf16[48,384]{1,0:T(8,128)(2,1)} async-done(((bf16[1536,384]{1,0:T(8,128)(2,1)}), bf16[48,384]{1,0:T(8,128)(2,1)}) %reduce-scatter.9.cloned.1.call-update) | async-done | bytes 36880 | tf_op jit(solution)/shard_map/reduce_scatter | solution.py:285
  (4249 shorter events, 1512.4 us)
Async XLA Ops:
  8.0 52.7 %all-gather.3.cloned.1.call-start = ((), (), s32[]{:S(2)}) async-start(), calls=%async_computation.4 | async-start | bytes 3538944 | tf_op jit(solution)/shard_map/all_gather | solution.py:191
  12.6 131.5 %reduce-scatter.7.cloned.1.call-start = ((), (), s32[]{:S(2)}) async-start(), calls=%async_computation.5 | async-start | bytes 7077888 | tf_op jit(solution)/shard_map/reduce_scatter | solution.py:194
  70.2 170.3 %all-reduce.5.cloned.1.call-start = ((), (), s32[]{:S(2)}) async-start(), calls=%async_computation.10 | async-start | bytes 327680
  74.8 1817.9 %all-gather.5.cloned.1.call-start = ((), (), s32[]{:S(2)}) async-start(), calls=%async_computation.6 | async-start | bytes 3538944 | tf_op jit(solution)/shard_map/all_gather | solution.py:270
  149.0 7.0 collective-permute-start.3
  156.7 2.8 collective-permute-start.4
  160.2 7.8 collective-permute-start.5
  168.0 8.9 collective-permute-start.6
  178.4 6.4 collective-permute-start.8
  184.8 7.0 collective-permute-start.9
  191.9 6.3 collective-permute-start.10
  198.3 2.0 collective-permute-start.11
  200.3 7.8 collective-permute-start.12
  208.2 5.5 collective-permute-start.13
  213.7 6.9 collective-permute-start.14
  222.2 19.1 collective-permute-start.15
  583.5 3.0 collective-permute-start
  586.8 5.5 collective-permute-start
  592.6 5.5 collective-permute-start
  598.4 5.5 collective-permute-start
  604.2 5.5 collective-permute-start
  610.0 6.0 collective-permute-start
  616.3 6.7 collective-permute-start
  1190.7 6.9 collective-permute-start.1
  1198.4 6.9 collective-permute-start.1
  1206.2 6.9 collective-permute-start.1
  1214.0 6.9 collective-permute-start.1
  1221.8 6.7 collective-permute-start.1
  1229.3 6.7 collective-permute-start.1
  1236.8 6.7 collective-permute-start.1
  1749.3 2.7 collective-permute-start.17
  1752.1 6.8 collective-permute-start.18
  1759.0 3.2 collective-permute-start.19
  1763.1 7.8 collective-permute-start.20
  1771.9 5.5 collective-permute-start.21
  1777.5 2.7 collective-permute-start.22
  1780.2 8.0 collective-permute-start.23
  1788.3 9.5 collective-permute-start.24
  1797.8 6.5 collective-permute-start.25
  1804.4 3.0 collective-permute-start.26
  1808.3 8.0 collective-permute-start.27
  1816.4 5.6 collective-permute-start.28
  1822.1 8.6 collective-permute-start.29
  1831.6 5.4 collective-permute-start.30
  1837.9 2.3 collective-permute-start.31
  1842.2 88.7 %reduce-scatter.13.cloned.1.call-start = ((), (), s32[]{:S(2)}) async-start(), calls=%async_computation.9 | async-start | bytes 368640
  1843.2 171.3 %reduce-scatter.11.cloned.1.call-start = ((), (), s32[]{:S(2)}) async-start(), calls=%async_computation.8 | async-start | bytes 1216512 | tf_op jit(solution)/shard_map/reduce_scatter | solution.py:288
  1897.9 201.1 %reduce-scatter.9.cloned.1.call-start = ((), (), s32[]{:S(2)}) async-start(), calls=%async_computation.7 | async-start | bytes 1216512 | tf_op jit(solution)/shard_map/reduce_scatter | solution.py:285
  (31 other events, 2018.9 us)
Sparse Core Ops, SparseCore 0:
  12.8 47.9 all-gather.2
  70.3 73.7 reduce-scatter.6
  1842.3 50.2 all-gather.4
  1895.0 35.8 reduce-scatter.12
  1934.6 79.7 reduce-scatter.10
  2018.1 80.8 reduce-scatter.8
Sparse Core Ops, SparseCore 1:
  74.9 107.8 all-reduce.4
where the time goes:
time: 2140 us; the launch traced here: 2110 us
  other arithmetic  813 us (38%)
  local copies, waits for them, and re-layouts  667 us (31%)
  waiting for transfers between devices  437 us (20%)
  starting transfers between devices  79.3 us (4%)
  between operations  60.3 us (3%)
  matrix products  46.8 us (2%)
    dynamic_slice x384, local copies, waits for them, and re-layouts, block_matrix(): lax.scan(block_one_frame, identity_map, (blank_score, label_score, active))  219 us
    another operation x386, local copies, waits for them, and re-layouts  187 us
    dynamic_update_slice x512, local copies, waits for them, and re-layouts, run_block(): lax.scan(run_one_frame, vector, (blank_score, label_score, active))[0]  173 us
    broadcast_in_dim x130, other arithmetic, run_block(): lax.scan(run_one_frame, vector, (blank_score, label_score, active))[0]  171 us
    reduce_sum x128, other arithmetic, lower_paths(): partial_sums[:, None] - partial_sums[None, :]  112 us
    dynamic_update_slice x128, other arithmetic, run_block(): lax.scan(run_one_frame, vector, (blank_score, label_score, active))[0]  84.6 us
    add_any x128, other arithmetic, advance(): vector[None, :]  84.1 us
    reduce_scatter x1, waiting for transfers between devices, on_device(): lax.psum_scatter(up_part.astype(jnp.bfloat16), 'joint', scatter_dimension...  83.2 us

commit v1 on v0

--- a/solution.py
+++ b/solution.py
@@ -188,7 +188,16 @@
     places = label_ids.shape[1] + 1
     own_rows = encoder_rows[0].astype(jnp.float32)
     normed_in = layer_norm(own_rows)[0].astype(jnp.bfloat16)
-    gathered = lax.all_gather(normed_in, "section", axis=0, tiled=True)
+    ways = lax.axis_size("section")
+    up = [(d, (d + 1) % ways) for d in range(ways)]
+    down = [(d, (d - 1) % ways) for d in range(ways)]
+    earlier, later = ([normed_in], [normed_in])
+    for _ in range(ways // 2):
+        earlier.append(lax.ppermute(earlier[-1], "section", up))
+    for _ in range((ways - 1) // 2):
+        later.append(lax.ppermute(later[-1], "section", down))
+    line = jnp.concatenate([*earlier[::-1], *later[1:]], axis=0)
+    gathered = jnp.roll(line, (lax.axis_index("section") - ways // 2) * normed_in.shape[0], axis=0)
     pre_hidden = jnp.dot(gathered, up_weight, preferred_element_type=jnp.float32)
     hidden = jax.nn.silu(pre_hidden).astype(jnp.bfloat16)
     encoded = own_rows + lax.psum_scatter(

time: 2140 us -> 2020 us (0.944)
  local copies, waits for them, and re-layouts: 667 us -> 538 us
  other arithmetic: 813 us -> 835 us
    another operation x386, local copies, waits for them, and re-layouts: 187 us -> 10.7 us
    all_gather x1 -> x0, waiting for transfers between devices: 48 us -> none  [on_device(): gathered = lax.all_gather(normed_in, 'section', axis=0, tiled=True)]
    dynamic_slice x384, local copies, waits for them, and re-layouts: 219 us -> 255 us  [block_matrix(): lax.scan(block_one_frame, identity_map, (blank_score, label_score, active))]
    ppermute x0 -> x7, waiting for transfers between devices: none -> 35.7 us  [the longest x4 35.7 us: on_device(): earlier.append(lax.ppermute(earlier[-1], 'section', up))]
where the time goes in v1:
time: 2020 us; the launch traced here: 2000 us
  other arithmetic  835 us (41%)
  local copies, waits for them, and re-layouts  538 us (27%)
  waiting for transfers between devices  424 us (21%)
  starting transfers between devices  89.9 us (4%)
  between operations  60.1 us (3%)
  matrix products  45.3 us (2%)
    dynamic_slice x384, local copies, waits for them, and re-layouts, block_matrix(): lax.scan(block_one_frame, identity_map, (blank_score, label_score, active))  255 us
    dynamic_update_slice x512, local copies, waits for them, and re-layouts, run_block(): lax.scan(run_one_frame, vector, (blank_score, label_score, active))[0]  174 us
    broadcast_in_dim x130, other arithmetic, run_block(): lax.scan(run_one_frame, vector, (blank_score, label_score, active))[0]  168 us
    reduce_sum x128, other arithmetic, lower_paths(): partial_sums[:, None] - partial_sums[None, :]  112 us
    select_n x128, other arithmetic, block_one_frame(): return (jnp.where(live_flag, moved, carried), None)  96.9 us
    abs x128, other arithmetic, advance(): jax.nn.logsumexp(lower_paths(label_row) + vector[None, :], axis=1)  89.9 us
    dynamic_update_slice x128, other arithmetic, run_block(): lax.scan(run_one_frame, vector, (blank_score, label_score, active))[0]  84.6 us
    reduce_scatter x1, waiting for transfers between devices, on_device(): lax.psum_scatter(up_part.astype(jnp.bfloat16), 'joint', scatter_dimension...  83.1 us

profile of v1, /device:TPU:2, one launch (start us, length us, event | category | flops | bytes accessed | tf_op | source)
XLA Modules:
  0.0 1997.6 jit_solution(4881383716045071198)
XLA Ops:
  13.9 13.1 collective-permute-done.2
  26.9 3.2 collective-permute-start.6
  30.2 8.3 collective-permute-done.3
  38.4 3.2 collective-permute-start.7
  41.7 7.5 collective-permute-done.4
  49.2 3.2 collective-permute-start.8
  52.4 6.9 collective-permute-done.5
  72.0 4.5 convolution_multiply_fusion
  93.1 57.8 %reduce-scatter.7.cloned.1.call-done = f32[128,1536]{1,0:T(8,128)} async-done(((f32[1024,1536]{1,0:T(8,128)}), f32[128,1536]{1,0:T(8,128)}) %reduce-scatter.7.cloned.1.call-update) | async-done | bytes 786448 | tf_op jit(solution)/shard_map/reduce_scatter | solution.py:203
  170.8 3.9 collective-permute-done.12
  185.1 4.8 collective-permute-done.15
  192.4 4.6 collective-permute-done.16
  204.0 3.1 collective-permute-start.19
  230.7 3.4 broadcast_in_dim.222
  234.1 6.8 broadcast_in_dim.223
  245.8 9.4 exponential_reduce_fusion.3
  255.2 18.4 reshape.609
  274.6 5.5 gather_fusion.31
  280.8 252.4 %while.74 = (s32[]{:T(128)}, f32[4,4]{1,0:T(4,128)S(1)}, pred[128]{0:T(512)(128)(4,1)S(1)}, f32[128,4]{1,0:T(8,128)S(1)}, f32[128,3]{1,0:T(8,128)S(1)}, /*index=5*/s32[]{:T(128)}, f32[]{:T(128)}, f32[1]{0:T(128)}) while((s32[]{:T(128)}, f32[4,4]{1,0:T(4,128)S(1)}, pred[128]{0:T(512)(128)(4,1)S(1)}, f32[128,4]{1,0:T(8,128)S(1)}, ...), condition=%wide.region_12.13_spmd, body=%wide.region_8.12_spmd.sunk | while | flops 476 | bytes 1144 | solution.py:68
  533.2 39.8 %while.75 = (s32[]{:T(128)}, f32[4]{0:T(128)S(1)}, pred[]{:T(512)}, f32[4,4]{1,0:T(4,128)S(1)}, s32[]{:T(128)}) while((s32[]{:T(128)}, f32[4]{0:T(128)S(1)}, pred[]{:T(512)}, f32[4,4]{1,0:T(4,128)S(1)}, s32[]{:T(128)}) %tuple.158), condition=%wide.region_16.17_spmd.clone, body=%wide.region_13.16_spmd.clone.sunk | while | flops 110 | bytes 486 | solution.py:255
  536.9 4.2 collective-permute-start
  542.7 4.2 collective-permute-start
  548.5 4.2 collective-permute-start
  554.3 4.2 collective-permute-start
  560.1 4.7 collective-permute-start
  566.4 5.4 collective-permute-start
  573.1 511.7 %while.78 = (s32[]{:T(128)}, f32[4]{0:T(128)S(1)}, f32[128,4,4]{2,1,0:T(4,128)}, pred[128,4]{1,0:T(8,128)(4,1)}, f32[128,4]{1,0:T(8,128)S(1)}, /*index=5*/pred[1...) while((s32[]{:T(128)}, f32[4]{0:T(128)S(1)}, ...), condition=%wide.region_21.22_spmd.clone.clone, body=%wide.region_17.21_spmd.clone.clone.sunk | while | flops 296 | bytes 5132 | solution.py:52
  1084.7 53.6 %while.76 = (s32[]{:T(128)}, f32[4]{0:T(128)S(1)}, pred[]{:T(512)}, f32[4,4]{1,0:T(4,128)S(1)}, s32[]{:T(128)}, /*index=5*/s32[]{:T(128)}) while((s32[]{:T(128)}, f32[4]{0:T(128)S(1)}, pred[]{:T(512)}, f32[4,4]{1,0:T(4,128)S(1)}, s32[]{:T(128)}, /*index=5*/s32[]{:T(128)}) %tuple.182), condition=%wide.region_25.26_spmd.clone, body=%wide.region_22.25_spmd.clone.sunk | while | flops 110 | bytes 498 | solution.py:261
  1086.2 5.6 collective-permute-done.1
  1094.0 5.6 collective-permute-done.1
  1101.8 5.6 collective-permute-done.1
  1109.5 5.6 collective-permute-done.1
  1117.3 5.4 collective-permute-done.1
  1124.8 5.4 collective-permute-done.1
  1132.3 5.4 collective-permute-done.1
  1141.7 486.3 %while.77 = (s32[]{:T(128)}, f32[4]{0:T(128)S(1)}, f32[128,4]{1,0:T(8,128)S(1)}, f32[128,3]{1,0:T(8,128)S(1)}, pred[128]{0:T(512)(128)(4,1)S(1)}, /*index=5*/pre...) while((s32[]{:T(128)}, f32[4]{0:T(128)S(1)}, ...), condition=%wide.region_33.34_spmd.clone, body=%wide.region_28.33_spmd.clone.sunk | while | flops 133 | bytes 553 | solution.py:52
  1628.3 12.2 fusion.34
  1651.5 3.3 collective-permute-done.25
  1657.7 2.9 collective-permute-start.27
  1681.5 3.0 collective-permute-start.31
  1698.2 3.4 collective-permute-start.34
  1713.2 5.0 collective-permute-start.36
  1734.2 48.0 %all-gather.2.cloned.1.call-done = bf16[1024,1536]{1,0:T(8,128)(2,1)} async-done(((bf16[128,1536]{1,0:T(8,128)(2,1)}), bf16[1024,1536]{1,0:T(8,128)(2,1)}) %all-gather.2.cloned.1.call-update) | async-done | bytes 3145744 | tf_op jit(solution)/shard_map/all_gather | solution.py:279
  1782.1 5.3 fusion.30
  1787.8 7.8 convolution_convert_fusion
  1795.6 24.9 %reduce-scatter.13.cloned.1.call-done = f32[80,4]{1,0:T(8,128)} async-done(((f32[640,4]{1,0:T(8,128)}), f32[80,4]{1,0:T(8,128)}) %reduce-scatter.13.cloned.1.call-update) | async-done | bytes 1296
  1822.0 82.1 %reduce-scatter.11.cloned.1.call-done = bf16[384,48]{0,1:T(8,128)(2,1)} async-done(((bf16[384,1536]{0,1:T(8,128)(2,1)}), bf16[384,48]{0,1:T(8,128)(2,1)}) %reduce-scatter.11.cloned.1.call-update) | async-done | bytes 36880 | tf_op jit(solution)/shard_map/reduce_scatter | solution.py:297
  1905.5 83.1 %reduce-scatter.9.cloned.1.call-done = bf16[48,384]{1,0:T(8,128)(2,1)} async-done(((bf16[1536,384]{1,0:T(8,128)(2,1)}), bf16[48,384]{1,0:T(8,128)(2,1)}) %reduce-scatter.9.cloned.1.call-update) | async-done | bytes 36880 | tf_op jit(solution)/shard_map/reduce_scatter | solution.py:294
  (4289 shorter events, 1417.7 us)
Async XLA Ops:
  8.0 142.9 %reduce-scatter.7.cloned.1.call-start = ((), (), s32[]{:S(2)}) async-start(), calls=%async_computation.4 | async-start | bytes 7077888 | tf_op jit(solution)/shard_map/reduce_scatter | solution.py:203
  11.9 15.0 collective-permute-start.2
  26.9 11.5 collective-permute-start.3
  26.9 11.5 collective-permute-start.6
  38.4 10.7 collective-permute-start.4
  38.4 10.7 collective-permute-start.7
  49.2 10.1 collective-permute-start.5
  49.2 13.5 collective-permute-start.8
  76.5 165.7 %all-reduce.5.cloned.1.call-start = ((), (), s32[]{:S(2)}) async-start(), calls=%async_computation.9 | async-start | bytes 327680
  81.0 1701.1 %all-gather.2.cloned.1.call-start = ((), (), s32[]{:S(2)}) async-start(), calls=%async_computation.5 | async-start | bytes 3538944 | tf_op jit(solution)/shard_map/all_gather | solution.py:279
  157.1 7.1 collective-permute-start.10
  166.4 8.3 collective-permute-start.12
  174.7 7.3 collective-permute-start.13
  183.6 6.4 collective-permute-start.15
  190.0 7.0 collective-permute-start.16
  197.0 5.4 collective-permute-start.17
  204.0 7.8 collective-permute-start.19
  211.8 5.5 collective-permute-start.20
  217.3 6.9 collective-permute-start.21
  224.3 18.6 collective-permute-start.22
  533.6 3.0 collective-permute-start
  536.9 5.5 collective-permute-start
  542.7 5.5 collective-permute-start
  548.5 5.5 collective-permute-start
  554.3 5.5 collective-permute-start
  560.1 5.9 collective-permute-start
  566.4 6.7 collective-permute-start
  1084.9 6.9 collective-permute-start.1
  1092.7 6.9 collective-permute-start.1
  1100.5 6.9 collective-permute-start.1
  1108.2 6.9 collective-permute-start.1
  1116.0 6.7 collective-permute-start.1
  1123.5 6.7 collective-permute-start.1
  1131.0 6.7 collective-permute-start.1
  1648.1 6.7 collective-permute-start.25
  1657.7 8.2 collective-permute-start.27
  1665.9 6.0 collective-permute-start.28
  1674.8 6.7 collective-permute-start.30
  1681.5 7.3 collective-permute-start.31
  1688.9 5.5 collective-permute-start.32
  1694.4 2.8 collective-permute-start.33
  1698.2 8.3 collective-permute-start.34
  1706.6 6.6 collective-permute-start.35
  1713.2 8.5 collective-permute-start.36
  1722.7 5.4 collective-permute-start.37
  1733.1 87.4 %reduce-scatter.13.cloned.1.call-start = ((), (), s32[]{:S(2)}) async-start(), calls=%async_computation.8 | async-start | bytes 368640
  1734.1 170.0 %reduce-scatter.11.cloned.1.call-start = ((), (), s32[]{:S(2)}) async-start(), calls=%async_computation.7 | async-start | bytes 1216512 | tf_op jit(solution)/shard_map/reduce_scatter | solution.py:297
  1787.5 201.2 %reduce-scatter.9.cloned.1.call-start = ((), (), s32[]{:S(2)}) async-start(), calls=%async_computation.6 | async-start | bytes 1216512 | tf_op jit(solution)/shard_map/reduce_scatter | solution.py:294
  (44 other events, 3809.2 us)
Sparse Core Ops, SparseCore 0:
  76.6 74.3 reduce-scatter.6
  1733.3 48.8 all-gather.1
  1784.7 35.8 reduce-scatter.12
  1824.3 79.7 reduce-scatter.10
  1907.8 80.8 reduce-scatter.8
Sparse Core Ops, SparseCore 1:
  81.1 108.4 all-reduce.4
